TPU v7x, 128 devices: a whole 4x4x4 slice. The times are simulated.
128 devices in a mesh: req: 32 (over z, x, core), mlp: 4 (over y).
Axes of the slice: x: 4, y: 4, z: 4, core: 2. Of those that a mesh axis runs over, the one named last changes fastest.
Arguments:
- tokens: bfloat16 [12288, 2048], P(('req', 'mlp')), may hold values from -6 to 6
- lengths: int32 [4], replicated, may hold values from 1 to 6144, 12288 in all
- in_gain: float32 [2048], replicated, may hold values from 0.5 to 1.5
- w_query: bfloat16 [2048, 2048], P(None, 'mlp'), may hold values from -0.125 to 0.125
- w_key: bfloat16 [2048, 2048], P(None, 'mlp'), may hold values from -1 to 1
- w_value: bfloat16 [2048, 4096], P(None, 'mlp'), may hold values from -0.125 to 0.125
- w_gate: bfloat16 [2048, 4096], P(None, 'mlp'), may hold values from -0.125 to 0.125
- w_beta: bfloat16 [2048, 16], P(None, 'mlp'), may hold values from -0.125 to 0.125
- w_decay: bfloat16 [2048, 16], P(None, 'mlp'), may hold values from -0.125 to 0.125
- decay_log: float32 [16], P('mlp'), may hold values from -11 to 0
- decay_bias: float32 [16], P('mlp'), may hold values from -3 to 1
- conv_query: float32 [4, 2048], P(None, 'mlp'), may hold values from -2.5 to 2.5
- conv_key: float32 [4, 2048], P(None, 'mlp'), may hold values from -2.5 to 2.5
- conv_value: float32 [4, 4096], P(None, 'mlp'), may hold values from -2.5 to 2.5
- head_gain: float32 [256], replicated, may hold values from 0.5 to 1.5
- w_out: bfloat16 [4096, 2048], P('mlp'), may hold values from -0.09375 to 0.09375
- mlp_gain: float32 [2048], replicated, may hold values from 0.5 to 1.5
- w_up_gate: bfloat16 [2048, 5632], P('req', 'mlp'), may hold values from -0.125 to 0.125
- w_up: bfloat16 [2048, 5632], P('req', 'mlp'), may hold values from -0.125 to 0.125
- w_down: bfloat16 [5632, 2048], P('mlp', 'req'), may hold values from -0.078125 to 0.078125
Outputs:
- layer_out: bfloat16 [12288, 2048], P(('req', 'mlp'))
Inputs may be any that keep to these rules, and one draw needn't show every extreme that they name: The 4 prompts lie end to end in the order given and their lengths sum to 12288; the longest has exactly 6144 tokens.
All inputs are finite; a program needn't handle non-finite values.
Results may differ from a plain program's by a relative error of at most 0.017.
Values may be sent and summed in bfloat16 or wider, within the bound.
No kernel may reach another device: no remote copies, remote signals or barrier semaphores. Data moves between devices by JAX's collectives and lax.ppermute only.
A program may use at most 128 MiB of HBM per device.

v0:
```python
import jax
import jax.numpy as jnp
from jax import lax
from jax.sharding import PartitionSpec as P

GROUP = 64
maximal_matmul_accuracy = lax.Precision.HIGHEST


def shifted(value, axis, steps):
    count = lax.axis_size(axis)
    first, last = (max(0, -steps), min(count, count - steps))
    return lax.ppermute(value, axis, [(source, source + steps) for source in range(first, last)])


def carried_in(shard, axis, combine, identity):
    length, index = (lax.axis_size(axis), lax.axis_index(axis))
    everything = jax.tree.map(
        lambda part, kind: lax.all_gather(part.astype(kind), axis),
        shard,
        jax.tree.map(lambda a: jnp.bfloat16 if a.dtype == jnp.float32 else a.dtype, shard),
    )
    start = jax.tree.map(
        lambda part, zero: jnp.broadcast_to(jnp.asarray(zero, part.dtype), part.shape),
        shard,
        identity,
    )

    def step(k, before):
        reached = k < index
        new = combine(
            before, jax.tree.map(lambda part, own: part[k].astype(own.dtype), everything, shard)
        )
        return jax.tree.map(lambda a, b: jnp.where(reached, a, b), new, before)

    return lax.fori_loop(0, length, step, start)


def rms_scale(values, gain):
    mean_square = jnp.mean(values * values, axis=-1, keepdims=True)
    return values / jnp.sqrt(mean_square + 1e-06) * gain


def unit_norm(values):
    return values / jnp.sqrt(jnp.sum(values * values, axis=-1, keepdims=True) + 1e-06)


def segment_of(positions, lengths):
    bounds = jnp.cumsum(lengths)[:-1]
    return jnp.sum((positions[:, None] >= bounds[None, :]).astype(jnp.int32), axis=1)


def causal_conv(projected, rim_rows, kernel, segment_ids, rim_segments):
    taps_count = kernel.shape[0]
    row_count = projected.shape[0]
    extended = jnp.concatenate([rim_rows, projected], axis=0).astype(jnp.float32)
    extended_ids = jnp.concatenate([rim_segments, segment_ids], axis=0)
    accumulated = jnp.zeros(projected.shape, jnp.float32)
    for offset in range(taps_count):
        window = lax.slice_in_dim(extended, offset, offset + row_count, axis=0)
        window_ids = lax.slice_in_dim(extended_ids, offset, offset + row_count, axis=0)
        same_doc = (window_ids == segment_ids)[:, None]
        accumulated = accumulated + kernel[offset][None, :] * jnp.where(same_doc, window, 0.0)
    return accumulated


def group_parts(query_vecs, key_vecs, value_vecs, beta_vals, log_decay, segment_ids, prior_segment):
    group_rows = query_vecs.shape[0]
    value_dim = value_vecs.shape[-1]
    cumulative = jnp.cumsum(log_decay, axis=0)
    row_index = jnp.arange(group_rows)[:, None]
    col_index = jnp.arange(group_rows)[None, :]
    same_doc = segment_ids[:, None] == segment_ids[None, :]
    keep_mask = ((row_index >= col_index) & same_doc)[None, :, :]
    strict_mask = (row_index > col_index)[None, :, :]
    head_cumul = jnp.transpose(cumulative)
    gaps = head_cumul[:, :, None] - head_cumul[:, None, :]
    weights = jnp.where(keep_mask, jnp.exp(jnp.where(keep_mask, gaps, 0.0)), 0.0)
    open_mask = (segment_ids == prior_segment).astype(query_vecs.dtype)
    start_decay = jnp.exp(cumulative) * open_mask[:, None]
    key_dots = jnp.einsum("ihd,jhd->hij", key_vecs, key_vecs, precision=maximal_matmul_accuracy)
    coupling = jnp.where(
        strict_mask, jnp.transpose(beta_vals)[:, :, None] * weights * key_dots, 0.0
    )
    system = coupling + jnp.eye(group_rows, dtype=query_vecs.dtype)[None]
    targets = jnp.concatenate(
        [beta_vals[:, :, None] * value_vecs, (beta_vals * start_decay)[:, :, None] * key_vecs],
        axis=-1,
    )
    solved = jax.scipy.linalg.solve_triangular(
        system, jnp.transpose(targets, (1, 0, 2)), lower=True, unit_diagonal=True
    )
    starting_value_rows = solved[:, :, :value_dim]
    delta_correction = solved[:, :, value_dim:]
    query_dots = weights * jnp.einsum(
        "ihd,jhd->hij", query_vecs, key_vecs, precision=maximal_matmul_accuracy
    )
    query_begin_offset = query_vecs * start_decay[:, :, None]
    final_key_rows = key_vecs * jnp.transpose(weights[:, -1, :])[:, :, None]
    carried_decay_factor = start_decay[-1]
    return (
        starting_value_rows,
        delta_correction,
        query_dots,
        query_begin_offset,
        final_key_rows,
        carried_decay_factor,
    )


def group_step(running_state, parts):
    (
        starting_value_rows,
        delta_correction,
        query_dots,
        query_begin_offset,
        final_key_rows,
        carried_decay_factor,
    ) = parts
    fresh_state_update = starting_value_rows - jnp.einsum(
        "mxf,mft->mxt", delta_correction, running_state, precision=maximal_matmul_accuracy
    )
    output_rows = jnp.einsum(
        "fob,obt->fot", query_begin_offset, running_state, precision=maximal_matmul_accuracy
    )
    output_rows = output_rows + jnp.einsum(
        "hij,hjv->ihv", query_dots, fresh_state_update, precision=maximal_matmul_accuracy
    )
    updated_state = carried_decay_factor[:, None, None] * running_state + jnp.einsum(
        "new,enr->ewr", final_key_rows, fresh_state_update, precision=maximal_matmul_accuracy
    )
    return (updated_state, output_rows)


def combine_maps(earlier, later):
    earlier_map, preceding_additive = earlier
    following_linear_map, following_additive = later
    joined_map = jnp.einsum(
        "hkl,hlm->hkm", following_linear_map, earlier_map, precision=maximal_matmul_accuracy
    )
    joined_add = (
        jnp.einsum(
            "baf,bfu->bau",
            following_linear_map,
            preceding_additive,
            precision=maximal_matmul_accuracy,
        )
        + following_additive
    )
    return (joined_map, joined_add)


def per_device(
    tokens,
    lengths,
    in_gain,
    w_query,
    w_key,
    w_value,
    w_gate,
    w_beta,
    w_decay,
    decay_log,
    decay_bias,
    conv_query,
    conv_key,
    conv_value,
    head_gain,
    w_out,
    mlp_gain,
    w_up_gate,
    w_up,
    w_down,
):
    share_rows = tokens.shape[0]
    gathered = lax.all_gather(tokens, "mlp", axis=0, tiled=True)
    piece_len = gathered.shape[0]
    head_count = w_beta.shape[1]
    key_dim = w_query.shape[1] // head_count
    value_dim = w_value.shape[1] // head_count
    taps_count = conv_query.shape[0]
    group_count = piece_len // GROUP
    piece_start = lax.axis_index("req") * piece_len
    positions = piece_start + jnp.arange(piece_len, dtype=jnp.int32)
    segment_ids = segment_of(positions, lengths)
    rim_segments = segment_of(
        piece_start - (taps_count - 1) + jnp.arange(taps_count - 1, dtype=jnp.int32), lengths
    )
    token_rows = gathered.astype(jnp.float32)
    normed = rms_scale(token_rows, in_gain).astype(jnp.bfloat16)
    proj_query = jnp.dot(normed, w_query, preferred_element_type=jnp.float32).astype(jnp.bfloat16)
    proj_key = jnp.dot(normed, w_key, preferred_element_type=jnp.float32).astype(jnp.bfloat16)
    proj_value = jnp.dot(normed, w_value, preferred_element_type=jnp.float32).astype(jnp.bfloat16)
    edge_rows = jnp.concatenate(
        [
            proj_query[piece_len - taps_count + 1 :],
            proj_key[piece_len - taps_count + 1 :],
            proj_value[piece_len - taps_count + 1 :],
        ],
        axis=1,
    )
    rim_all = shifted(edge_rows, "req", 1)
    query_width = proj_query.shape[1]
    key_width = proj_key.shape[1]
    rim_query = rim_all[:, :query_width]
    rim_key = rim_all[:, query_width : query_width + key_width]
    rim_value = rim_all[:, query_width + key_width :]
    conv_q = jax.nn.silu(causal_conv(proj_query, rim_query, conv_query, segment_ids, rim_segments))
    conv_k = jax.nn.silu(causal_conv(proj_key, rim_key, conv_key, segment_ids, rim_segments))
    conv_v = jax.nn.silu(causal_conv(proj_value, rim_value, conv_value, segment_ids, rim_segments))
    query_vecs = unit_norm(conv_q.reshape(piece_len, head_count, key_dim)) * key_dim ** (-0.5)
    key_vecs = unit_norm(conv_k.reshape(piece_len, head_count, key_dim))
    value_vecs = conv_v.reshape(piece_len, head_count, value_dim)
    gate_lin = jnp.dot(normed, w_gate, preferred_element_type=jnp.float32).astype(jnp.bfloat16)
    beta_vals = jax.nn.sigmoid(jnp.dot(normed, w_beta, preferred_element_type=jnp.float32))
    log_decay = -jnp.exp(decay_log) * jax.nn.softplus(
        jnp.dot(normed, w_decay, preferred_element_type=jnp.float32) + decay_bias
    )

    def shaped(values):
        return values.reshape((group_count, GROUP) + values.shape[1:])

    prior_ids = segment_of(
        piece_start + jnp.arange(group_count, dtype=jnp.int32) * GROUP - 1, lengths
    )
    parts = jax.vmap(group_parts)(
        shaped(query_vecs),
        shaped(key_vecs),
        shaped(value_vecs),
        shaped(beta_vals),
        shaped(log_decay),
        shaped(segment_ids),
        prior_ids,
    )
    eye_block = jnp.broadcast_to(
        jnp.eye(key_dim, dtype=jnp.float32), (head_count, key_dim, key_dim)
    )
    zero_state = jnp.zeros((head_count, key_dim, value_dim), jnp.float32)

    def compose(carried, parts_one):
        (
            starting_value_rows,
            delta_correction,
            query_dots,
            query_begin_offset,
            final_key_rows,
            carried_decay_factor,
        ) = parts_one
        local_map = carried_decay_factor[:, None, None] * eye_block - jnp.einsum(
            "chk,hcl->hkl", final_key_rows, delta_correction, precision=maximal_matmul_accuracy
        )
        within_piece_additive = jnp.einsum(
            "new,enr->ewr", final_key_rows, starting_value_rows, precision=maximal_matmul_accuracy
        )
        return (combine_maps(carried, (local_map, within_piece_additive)), None)

    piece_maps, _ = lax.scan(compose, (eye_block, zero_state), parts)
    incoming = carried_in(piece_maps, "req", combine_maps, (eye_block, zero_state))
    _, output_rows = lax.scan(group_step, incoming[1], parts)
    output_rows = output_rows.reshape(piece_len, head_count, value_dim)
    gate_vals = jax.nn.silu(gate_lin.astype(jnp.float32)).reshape(piece_len, head_count, value_dim)
    head_out = (
        (rms_scale(output_rows, head_gain) * gate_vals)
        .reshape(piece_len, head_count * value_dim)
        .astype(jnp.bfloat16)
    )
    partial_out = jnp.dot(head_out, w_out, preferred_element_type=jnp.float32)
    attn_sum = lax.psum(partial_out.astype(jnp.bfloat16), "mlp").astype(jnp.float32)
    resid = token_rows + attn_sum
    mlp_in = rms_scale(resid, mlp_gain).astype(jnp.bfloat16)
    resid_mine = lax.dynamic_slice_in_dim(resid, lax.axis_index("mlp") * share_rows, share_rows, 0)

    def add_rows(piece):
        return jnp.dot(mlp_in, piece, preferred_element_type=jnp.float32)

    gate_acc = add_rows(lax.all_gather(w_up_gate, "req", axis=0, tiled=True))
    up_acc = add_rows(lax.all_gather(w_up, "req", axis=0, tiled=True))
    hidden = (jax.nn.silu(gate_acc) * up_acc).astype(jnp.bfloat16)
    down_terms = jnp.dot(
        hidden,
        lax.all_gather(w_down, "req", axis=1, tiled=True),
        preferred_element_type=jnp.float32,
    )
    mlp_share = lax.psum_scatter(
        down_terms.astype(jnp.bfloat16), "mlp", scatter_dimension=0, tiled=True
    ).astype(jnp.float32)
    return (resid_mine + mlp_share).astype(jnp.bfloat16)


def solution(mesh):
    placed = (
        P(("req", "mlp"), None),
        P(),
        P(),
        P(None, "mlp"),
        P(None, "mlp"),
        P(None, "mlp"),
        P(None, "mlp"),
        P(None, "mlp"),
        P(None, "mlp"),
        P("mlp"),
        P("mlp"),
        P(None, "mlp"),
        P(None, "mlp"),
        P(None, "mlp"),
        P(),
        P("mlp", None),
        P(),
        P("req", "mlp"),
        P("req", "mlp"),
        P("mlp", "req"),
    )
    return jax.shard_map(
        per_device, mesh=mesh, in_specs=placed, out_specs=P(("req", "mlp"), None), check_vma=False
    )
```

profile of v0, /device:TPU:0, one launch (start us, length us, event | category | flops | bytes accessed | tf_op | source)
XLA Modules:
  0.0 670.5 jit_solution(12898045852853135112)
XLA Ops:
  15.9 22.1 %all-gather.9.cloned.1.call-done = bf16[384,2048]{1,0:T(8,128)(2,1)} async-done(((bf16[96,2048]{1,0:T(8,128)(2,1)}), bf16[384,2048]{1,0:T(8,128)(2,1)}) %all-gather.9.cloned.1.call-update) | async-done | bytes 1572880 | tf_op jit(solution)/shard_map/all_gather | solution.py:176
  40.5 4.6 convolution_convert_fusion.3
  55.8 2.7 fusion.94
  61.0 2.8 fusion.64
  63.8 119.3 %custom-call.4 = f32[6,4,1,64,64]{3,4,2,1,0:T(8,128)} custom-call(f32[6,4,1,64,64]{4,3,2,1,0:T(8,128)} %fusion.64), custom_call_target="InvertDiagBlocksLowerTriangular" | custom-call | tf_op jit(solution)/shard_map/vmap(jit(_solve_triangular))/vmap()/triangular_solve | solution.py:90
  183.4 2.3 divide_multiply_fusion
  185.8 2.9 reshape_reshape.3
  194.9 23.6 %while.40 = (s32[]{:T(128)}, f32[4,128,128]{2,1,0:T(8,128)S(1)}, f32[4,128,256]{2,1,0:T(8,128)S(1)}, f32[6,4]{1,0:T(8,128)}, f32[6,64,4,128]{3,1,2,0:T(8,128)S(1...) while((s32[]{:T(128)}, f32[4,128,128]{2,1,0:T(8,128)S(1)}, ...), condition=%wide.region_8.9_spmd.clone, body=%wide.region_7.8_spmd.clone.sunk | while | flops 453378048 | bytes 4655763 | solution.py:257
  220.5 2.4 mul.377
  225.9 2.6 broadcast_multiply_fusion
  228.5 2.6 convolution_multiply_fusion.1
  231.1 35.7 %all-gather.17.cloned.1.call-done = bf16[128,128,128]{2,1,0:T(8,128)(2,1)} async-done(((bf16[4,128,128]{2,1,0:T(8,128)(2,1)}), bf16[128,128,128]{2,1,0:T(8,128)(2,1)}) %all-gather.17.cloned.1.call-update) | async-done | bytes 4194320 | tf_op jit(solution)/shard_map/all_gather | solution.py:19
  266.8 54.4 %all-gather.19.cloned.1.call-done = bf16[128,128,256]{2,1,0:T(8,128)(2,1)} async-done(((bf16[4,128,256]{2,1,0:T(8,128)(2,1)}), bf16[128,128,256]{2,1,0:T(8,128)(2,1)}) %all-gather.19.cloned.1.call-update) | async-done | bytes 8388624 | tf_op jit(solution)/shard_map/all_gather | solution.py:19
  321.3 50.3 %while.41 = (s32[]{:T(128)}, f32[4,128,256]{2,1,0:T(8,128)S(1)}, s32[]{:T(128)}, bf16[32,4,128,128]{3,2,1,0:T(8,128)(2,1)}, bf16[32,4,128,256]{3,2,1,0:T(8,128)(2,1)}, /*index=5*/s32[]{:T(128)}, s32[]{:T(128)}) while((s32[]{:T(128)}, f32[4,128,256]{2,1,0:T(8,128)S(1)}, s32[]{:T(128)}, bf16[32,4,128,128]{3,2,1,0:T(8,128)(2,1)}, ...), condition=%wide.region_10.11_spmd.clone, body=%wide.region_9.10_spmd.clone.sunk | while | flops 201981952 | bytes 3017311 | solution.py:36
  371.6 36.9 %while.39 = (s32[]{:T(128)}, f32[4,128,256]{2,1,0:T(8,128)S(1)}, f32[6,64,4,256]{3,1,2,0:T(8,128)}, f32[6,4]{1,0:T(8,128)}, f32[6,64,4,128]{3,1,2,0:T(8,128)S(1)...) while((s32[]{:T(128)}, f32[4,128,256]{2,1,0:T(8,128)S(1)}, ...), condition=%wide.region_13.14_spmd, body=%wide.region_12.13_spmd.sunk | while | flops 352714752 | bytes 4459661 | solution.py:259
  416.6 9.2 %convolution_convert_fusion.1 = bf16[384,2048]{1,0:T(8,128)(2,1)} fusion(bf16[1024,2048]{1,0:T(8,128)(2,1)} %param.41, f32[384,1024]{1,0:T(8,128)} %bitcast.169, f32[384,1024]{1,0:T(8,128)} %bitcast.168, bf16[384,2048]{1,0:T(8,128)(2,1)S(1)} %copy-done.5, bf16[2048,1024]{1,0:T(8,128)(2,1)} %param.32, f32[1024]{0:T(1024)S(1)} %bitcast.191), kind=kOutput, calls=%fused_computation.61 | convolution fusion | flops 3225944064 | bytes 14684160 | tf_op jit(solution)/shard_map/dot_general | solution.py:267
  428.0 47.9 %all-reduce.2.cloned.1.call-done = bf16[384,2048]{1,0:T(8,128)(2,1)} async-done(((bf16[384,2048]{1,0:T(8,128)(2,1)}), bf16[384,2048]{1,0:T(8,128)(2,1)}) %all-reduce.2.cloned.1.call-update) | async-done | bytes 1572880 | tf_op jit(solution)/shard_map/psum | solution.py:268
  475.9 3.5 convert_add_fusion
  479.4 46.8 %all-gather.11.cloned.1.call-done = bf16[2048,1408]{1,0:T(8,128)(2,1)} async-done(((bf16[64,1408]{1,0:T(8,128)(2,1)}), bf16[2048,1408]{1,0:T(8,128)(2,1)}) %all-gather.11.cloned.1.call-update) | async-done | bytes 5767184 | tf_op jit(solution)/shard_map/all_gather | solution.py:276
  526.2 7.2 %fusion.93 = f32[384,1408]{1,0:T(8,128)} fusion(bf16[2048,1408]{1,0:T(8,128)(2,1)} %all-gather.11.cloned.1.call-done, f32[2048]{0:T(1024)S(1)} %copy-done.42, f32[384]{0:T(512)S(1)} %add_sqrt_fusion.3, bf16[384,2048]{1,0:T(8,128)(2,1)} %all-reduce.2.cloned.1.call-done, bf16[384,2048]{1,0:T(8,128)(2,1)S(1)} %copy-done.3), kind=kOutput, calls=%fused_computation.178 | convolution fusion | flops 2219311104 | bytes 11085312 | tf_op jit(solution)/shard_map/dot_general | solution.py:274
  533.4 42.2 %all-gather.13.cloned.1.call-done = bf16[2048,1408]{1,0:T(8,128)(2,1)} async-done(((bf16[64,1408]{1,0:T(8,128)(2,1)}), bf16[2048,1408]{1,0:T(8,128)(2,1)}) %all-gather.13.cloned.1.call-update) | async-done | bytes 5767184 | tf_op jit(solution)/shard_map/all_gather | solution.py:277
  575.5 49.5 %all-gather.15.cloned.1.call-done = bf16[1408,2048]{0,1:T(8,128)(2,1)} async-done(((bf16[1408,64]{0,1:T(8,128)(2,1)}), bf16[1408,2048]{0,1:T(8,128)(2,1)}) %all-gather.15.cloned.1.call-update) | async-done | bytes 5767184 | tf_op jit(solution)/shard_map/all_gather | solution.py:281
  625.0 11.8 %convolution_convert_fusion = bf16[384,2048]{1,0:T(8,128)(2,1)} fusion(bf16[1408,2048]{0,1:T(8,128)(2,1)} %all-gather.15.cloned.1.call-done, bf16[2048,1408]{1,0:T(8,128)(2,1)} %all-gather.13.cloned.1.call-done, f32[384,1408]{1,0:T(8,128)} %fusion.93, f32[2048]{0:T(1024)S(1)} %copy-done.42, f32[384]{0:T(512)S(1)} %add_sqrt_fusion.3, ...), kind=kOutput, calls=%fused_computation.60 | convolution fusion | flops 4437934080 | bytes 18425344 | tf_op jit(solution)/shard_map/dot_general | solution.py:279
  636.8 24.7 %reduce-scatter.2.cloned.1.call-done = bf16[96,2048]{1,0:T(8,128)(2,1)} async-done(((bf16[384,2048]{1,0:T(8,128)(2,1)}), bf16[96,2048]{1,0:T(8,128)(2,1)}) %reduce-scatter.2.cloned.1.call-update) | async-done | bytes 393232 | tf_op jit(solution)/shard_map/reduce_scatter | solution.py:284
  (318 shorter events, 157.1 us)
Async XLA Ops:
  6.5 38.6 %copy-start = (bf16[2048,512]{1,0:T(8,128)(2,1)S(1)}, bf16[2048,512]{1,0:T(8,128)(2,1)}, u32[]{:S(2)}) copy-start(bf16[2048,512]{1,0:T(8,128)(2,1)} %param.29) | copy-start | bytes 6291460
  6.5 33.4 %copy-start.25 = (f32[2048]{0:T(1024)S(1)}, f32[2048]{0:T(1024)}, u32[]{:S(2)}) copy-start(f32[2048]{0:T(1024)} %param.28) | copy-start | bytes 24580
  6.5 31.5 %all-gather.9.cloned.1.call-start = ((), (), s32[]{:S(2)}) async-start(), calls=%async_computation.1 | async-start | bytes 1966080 | tf_op jit(solution)/shard_map/all_gather | solution.py:176
  7.3 259.6 %all-gather.17.cloned.1.call-start = ((), (), s32[]{:S(2)}) async-start(), calls=%async_computation.7 | async-start | bytes 4325376 | tf_op jit(solution)/shard_map/all_gather | solution.py:19
  40.5 9.1 %copy-start.4 = (bf16[384,2048]{1,0:T(8,128)(2,1)}, bf16[384,2048]{1,0:T(8,128)(2,1)S(1)}, u32[]{:S(2)}) copy-start(bf16[384,2048]{1,0:T(8,128)(2,1)S(1)} %fusion.44) | copy-start | bytes 4718596
  47.0 2.7 copy-start.21
  47.0 2.7 copy-start.40
  48.0 2.7 copy-start.22
  48.0 6.3 collective-permute-start
  60.9 2.9 copy-start.11
  61.0 122.2 %copy-start.15 = (bf16[384,1024]{1,0:T(8,128)(2,1)S(1)}, bf16[384,1024]{1,0:T(8,128)(2,1)}, u32[]{:S(2)}) copy-start(bf16[384,1024]{1,0:T(8,128)(2,1)} %copy-done.14) | copy-start | bytes 2359300
  63.8 119.6 %copy-start.23 = (f32[1,1024]{1,0:T(1,128)S(1)}, f32[1,1024]{1,0:T(1,128)}, u32[]{:S(2)}) copy-start(f32[1,1024]{1,0:T(1,128)} %get-tuple-element.401) | copy-start | bytes 12292
  63.8 119.6 %copy-start.24 = (f32[1,1024]{1,0:T(1,128)S(1)}, f32[1,1024]{1,0:T(1,128)}, u32[]{:S(2)}) copy-start(f32[1,1024]{1,0:T(1,128)} %get-tuple-element.402) | copy-start | bytes 12292
  185.8 2.9 copy-start.12
  219.3 102.0 %all-gather.19.cloned.1.call-start = ((), (), s32[]{:S(2)}) async-start(), calls=%async_computation.8 | async-start | bytes 8650752 | tf_op jit(solution)/shard_map/all_gather | solution.py:19
  220.1 255.8 %all-reduce.2.cloned.1.call-start = ((), (), s32[]{:S(2)}) async-start(), calls=%async_computation.2 | async-start | bytes 3145728 | tf_op jit(solution)/shard_map/psum | solution.py:268
  220.5 4.2 copy-start.9
  425.7 50.1 %copy-start.3 = (bf16[384,2048]{1,0:T(8,128)(2,1)S(1)}, bf16[384,2048]{1,0:T(8,128)(2,1)}, u32[]{:S(2)}) copy-start(bf16[384,2048]{1,0:T(8,128)(2,1)} %all-gather.9.cloned.1.call-done) | copy-start | bytes 4718596
  425.8 100.4 %all-gather.11.cloned.1.call-start = ((), (), s32[]{:S(2)}) async-start(), calls=%async_computation.3 | async-start | bytes 5947392 | tf_op jit(solution)/shard_map/all_gather | solution.py:276
  426.4 149.2 %all-gather.13.cloned.1.call-start = ((), (), s32[]{:S(2)}) async-start(), calls=%async_computation.4 | async-start | bytes 5947392 | tf_op jit(solution)/shard_map/all_gather | solution.py:277
  426.9 198.1 %all-gather.15.cloned.1.call-start = ((), (), s32[]{:S(2)}) async-start(), calls=%async_computation.5 | async-start | bytes 5947392 | tf_op jit(solution)/shard_map/all_gather | solution.py:281
  427.7 98.5 %copy-start.42 = (f32[2048]{0:T(1024)S(1)}, f32[2048]{0:T(1024)}, u32[]{:S(2)}) copy-start(f32[2048]{0:T(1024)} %param.42) | copy-start | bytes 24580
  427.7 233.8 %reduce-scatter.2.cloned.1.call-start = ((), (), s32[]{:S(2)}) async-start(), calls=%async_computation.6 | async-start | bytes 1966080 | tf_op jit(solution)/shard_map/reduce_scatter | solution.py:284
  636.7 26.9 %copy-start.1 = (bf16[2048,512]{1,0:T(8,128)(2,1)S(1)}, bf16[2048,512]{1,0:T(8,128)(2,1)}, u32[]{:S(2)}) copy-start(bf16[2048,512]{1,0:T(8,128)(2,1)} %param.29) | copy-start | bytes 6291460
  (28 other events, 53.9 us)
Sparse Core Ops, SparseCore 0:
  9.0 28.9 all-gather.8
  219.4 47.3 all-gather.16
  269.1 52.1 all-gather.18
  425.9 49.9 all-reduce.1
  478.0 48.1 all-gather.10
  528.3 47.1 all-gather.12
  577.8 47.1 all-gather.14
  636.9 24.5 reduce-scatter.1
where the time goes:
time: 673 us; the launch traced here: 670 us
  waiting for transfers between devices  326 us (48%)
  other arithmetic  148 us (22%)
  matrix products  144 us (21%)
  local copies, waits for them, and re-layouts  33.9 us (5%)
  between operations  14.3 us (2%)
    another operation x2, other arithmetic, group_parts(): jax.scipy.linalg.solve_triangular(system, jnp.transpose(targets, (1, 0, 2...  119 us
    all_gather x2, waiting for transfers between devices, carried_in(): lax.all_gather(part.astype(kind), axis)  90.2 us
    dot_general x38, matrix products, combine_maps(): jnp.einsum('baf,bfu->bau', following_linear_map, preceding_additive, prec...  51.6 us
    all_gather x1, waiting for transfers between devices, per_device(): lax.all_gather(w_down, 'req', axis=1, tiled=True)  49.5 us
    psum x1, waiting for transfers between devices, per_device(): lax.psum(partial_out.astype(jnp.bfloat16), 'mlp').astype(jnp.float32)  47.9 us
    all_gather x1, waiting for transfers between devices, per_device(): gate_acc = add_rows(lax.all_gather(w_up_gate, 'req', axis=0, tiled=True))  46.8 us
    all_gather x1, waiting for transfers between devices, per_device(): up_acc = add_rows(lax.all_gather(w_up, 'req', axis=0, tiled=True))  42.2 us
    reduce_scatter x1, waiting for transfers between devices, per_device(): lax.psum_scatter(down_terms.astype(jnp.bfloat16), 'mlp', scatter_dimensio...  24.7 us
  transfers between devices with their start and end apart: 9, of which 8 were waited for; matrix products, arithmetic and copies ran while one was open for 5% of the time, Pallas kernels for 0%

commit v1 on v0

--- a/solution.py
+++ b/solution.py
@@ -5,6 +5,12 @@
 
 GROUP = 64
 maximal_matmul_accuracy = lax.Precision.HIGHEST
+
+
+def in_order(blocks, dim):
+    blocks = jnp.moveaxis(blocks, 0, dim)
+    shape = blocks.shape
+    return blocks.reshape(*shape[:dim], shape[dim] * shape[dim + 1], *shape[dim + 2 :])
 
 
 def shifted(value, axis, steps):
@@ -173,7 +179,19 @@
     w_down,
 ):
     share_rows = tokens.shape[0]
-    gathered = lax.all_gather(tokens, "mlp", axis=0, tiled=True)
+    size = lax.axis_size("mlp")
+    pairs = [(i, (i + 1) % size) for i in range(size)]
+    back = [(b_2, a_2) for a_2, b_2 in pairs]
+    lower, upper = ([], [])
+    for step_2 in range(size - 1):
+        if step_2 % 2 == 0:
+            lower.append(lax.ppermute(lower[-1] if lower else tokens, "mlp", pairs))
+        else:
+            upper.append(lax.ppermute(upper[-1] if upper else tokens, "mlp", back))
+    blocks = jnp.stack([*lower[::-1], tokens, *upper])
+    shift = lax.axis_index("mlp") - len(lower)
+    blocks = blocks[(jnp.arange(size) - shift) % size]
+    gathered = in_order(blocks, 0)
     piece_len = gathered.shape[0]
     head_count = w_beta.shape[1]
     key_dim = w_query.shape[1] // head_count

time: 673 us -> 672 us (level)
  waiting for transfers between devices: 326 us -> 312 us
    all_gather x1 -> x0, waiting for transfers between devices: 22.1 us -> none  [per_device(): gathered = lax.all_gather(tokens, 'mlp', axis=0, tiled=True)]
    ppermute x0 -> x3, waiting for transfers between devices: none -> 11.3 us  [the longest x2 11.3 us: per_device(): lower.append(lax.ppermute(lower[-1] if lower else tokens, 'mlp', pairs))]
  transfers between devices with their start and end apart: 9 -> 11, of which waited for: 8 -> 9; matrix products, arithmetic and copies ran while one was open for 5% -> 6% of each run, Pallas kernels for 0% -> 0%
where the time goes in v1:
time: 672 us; the launch traced here: 669 us
  waiting for transfers between devices  312 us (46%)
  other arithmetic  154 us (23%)
  matrix products  144 us (21%)
  local copies, waits for them, and re-layouts  37.2 us (6%)
  between operations  14.3 us (2%)
    another operation x2, other arithmetic, group_parts(): jax.scipy.linalg.solve_triangular(system, jnp.transpose(targets, (1, 0, 2...  119 us
    all_gather x2, waiting for transfers between devices, carried_in(): lax.all_gather(part.astype(kind), axis)  90.4 us
    dot_general x38, matrix products, combine_maps(): jnp.einsum('baf,bfu->bau', following_linear_map, preceding_additive, prec...  51.6 us
    all_gather x1, waiting for transfers between devices, per_device(): lax.all_gather(w_down, 'req', axis=1, tiled=True)  49.3 us
    psum x1, waiting for transfers between devices, per_device(): lax.psum(partial_out.astype(jnp.bfloat16), 'mlp').astype(jnp.float32)  48 us
    all_gather x1, waiting for transfers between devices, per_device(): gate_acc = add_rows(lax.all_gather(w_up_gate, 'req', axis=0, tiled=True))  44.7 us
    all_gather x1, waiting for transfers between devices, per_device(): up_acc = add_rows(lax.all_gather(w_up, 'req', axis=0, tiled=True))  42.2 us
    reduce_scatter x1, waiting for transfers between devices, per_device(): lax.psum_scatter(down_terms.astype(jnp.bfloat16), 'mlp', scatter_dimensio...  24.8 us
  transfers between devices with their start and end apart: 11, of which 9 were waited for; matrix products, arithmetic and copies ran while one was open for 6% of the time, Pallas kernels for 0%

profile of v1, /device:TPU:0, one launch (start us, length us, event | category | flops | bytes accessed | tf_op | source)
XLA Modules:
  0.0 669.4 jit_solution(775620099718975421)
XLA Ops:
  19.5 11.1 %collective-permute-done.1 = bf16[96,2048]{1,0:T(8,128)(2,1)} collective-permute-done((bf16[96,2048]{1,0:T(8,128)(2,1)S(1)}, bf16[96,2048]{1,0:T(8,128)(2,1)}, u32[]{:S(2)}, u32[]{:S(2)}) %collective-permute-start.1) | collective-permute-done | bytes 393248 | tf_op jit(solution)/shard_map/ppermute | solution.py:188
  30.6 2.5 pad_maximum_fusion
  33.1 3.2 gather_fusion
  40.2 4.6 convolution_convert_fusion.3
  55.2 2.7 fusion.95
  60.4 2.8 fusion.64
  63.3 119.3 %custom-call.4 = f32[6,4,1,64,64]{3,4,2,1,0:T(8,128)} custom-call(f32[6,4,1,64,64]{4,3,2,1,0:T(8,128)} %fusion.64), custom_call_target="InvertDiagBlocksLowerTriangular" | custom-call | tf_op jit(solution)/shard_map/vmap(jit(_solve_triangular))/vmap()/triangular_solve | solution.py:96
  185.2 2.9 reshape_reshape.3
  194.4 23.6 %while.40 = (s32[]{:T(128)}, f32[4,128,128]{2,1,0:T(8,128)S(1)}, f32[4,128,256]{2,1,0:T(8,128)S(1)}, f32[6,4]{1,0:T(8,128)}, f32[6,64,4,128]{3,1,2,0:T(8,128)S(1...) while((s32[]{:T(128)}, f32[4,128,128]{2,1,0:T(8,128)S(1)}, ...), condition=%wide.region_8.9_spmd.clone, body=%wide.region_7.8_spmd.clone.sunk | while | flops 453378048 | bytes 4655763 | solution.py:275
  225.3 2.6 broadcast_multiply_fusion
  227.9 2.6 convolution_multiply_fusion.1
  230.5 36.0 %all-gather.14.cloned.1.call-done = bf16[128,128,128]{2,1,0:T(8,128)(2,1)} async-done(((bf16[4,128,128]{2,1,0:T(8,128)(2,1)}), bf16[128,128,128]{2,1,0:T(8,128)(2,1)}) %all-gather.14.cloned.1.call-update) | async-done | bytes 4194320 | tf_op jit(solution)/shard_map/all_gather | solution.py:25
  266.5 54.4 %all-gather.16.cloned.1.call-done = bf16[128,128,256]{2,1,0:T(8,128)(2,1)} async-done(((bf16[4,128,256]{2,1,0:T(8,128)(2,1)}), bf16[128,128,256]{2,1,0:T(8,128)(2,1)}) %all-gather.16.cloned.1.call-update) | async-done | bytes 8388624 | tf_op jit(solution)/shard_map/all_gather | solution.py:25
  320.9 50.3 %while.41 = (s32[]{:T(128)}, f32[4,128,256]{2,1,0:T(8,128)S(1)}, s32[]{:T(128)}, bf16[32,4,128,128]{3,2,1,0:T(8,128)(2,1)}, bf16[32,4,128,256]{3,2,1,0:T(8,128)(2,1)}, /*index=5*/s32[]{:T(128)}, s32[]{:T(128)}) while((s32[]{:T(128)}, f32[4,128,256]{2,1,0:T(8,128)S(1)}, s32[]{:T(128)}, bf16[32,4,128,128]{3,2,1,0:T(8,128)(2,1)}, ...), condition=%wide.region_10.11_spmd.clone, body=%wide.region_9.10_spmd.clone.sunk | while | flops 201981952 | bytes 3017311 | solution.py:42
  371.2 36.9 %while.39 = (s32[]{:T(128)}, f32[4,128,256]{2,1,0:T(8,128)S(1)}, f32[6,64,4,256]{3,1,2,0:T(8,128)}, f32[6,4]{1,0:T(8,128)}, f32[6,64,4,128]{3,1,2,0:T(8,128)S(1)...) while((s32[]{:T(128)}, f32[4,128,256]{2,1,0:T(8,128)S(1)}, ...), condition=%wide.region_13.14_spmd, body=%wide.region_12.13_spmd.sunk | while | flops 352714752 | bytes 4459661 | solution.py:277
  416.2 9.2 %convolution_convert_fusion.1 = bf16[384,2048]{1,0:T(8,128)(2,1)} fusion(bf16[1024,2048]{1,0:T(8,128)(2,1)} %param.41, f32[384,1024]{1,0:T(8,128)} %bitcast.188, f32[384,1024]{1,0:T(8,128)} %bitcast.187, bf16[384,2048]{1,0:T(8,128)(2,1)S(1)} %copy-done.4, bf16[2048,1024]{1,0:T(8,128)(2,1)} %param.32, f32[1024]{0:T(1024)S(1)} %bitcast.213), kind=kOutput, calls=%fused_computation.62 | convolution fusion | flops 3225944064 | bytes 14684160 | tf_op jit(solution)/shard_map/dot_general | solution.py:285
  427.5 48.0 %all-reduce.2.cloned.1.call-done = bf16[384,2048]{1,0:T(8,128)(2,1)} async-done(((bf16[384,2048]{1,0:T(8,128)(2,1)}), bf16[384,2048]{1,0:T(8,128)(2,1)}) %all-reduce.2.cloned.1.call-update) | async-done | bytes 1572880 | tf_op jit(solution)/shard_map/psum | solution.py:286
  475.5 3.7 bitcast_add_fusion
  481.1 44.7 %all-gather.8.cloned.1.call-done = bf16[2048,1408]{1,0:T(8,128)(2,1)} async-done(((bf16[64,1408]{1,0:T(8,128)(2,1)}), bf16[2048,1408]{1,0:T(8,128)(2,1)}) %all-gather.8.cloned.1.call-update) | async-done | bytes 5767184 | tf_op jit(solution)/shard_map/all_gather | solution.py:294
  525.8 7.1 %fusion.102 = f32[384,1408]{1,0:T(8,128)} fusion(bf16[384,2048]{1,0:T(8,128)(2,1)} %multiply_convert_fusion, bf16[2048,1408]{1,0:T(8,128)(2,1)} %all-gather.8.cloned.1.call-done), kind=kOutput, calls=%fused_computation.194 | convolution fusion | flops 2214592512 | bytes 9502720 | tf_op jit(solution)/shard_map/dot_general | solution.py:292
  532.9 42.2 %all-gather.10.cloned.1.call-done = bf16[2048,1408]{1,0:T(8,128)(2,1)} async-done(((bf16[64,1408]{1,0:T(8,128)(2,1)}), bf16[2048,1408]{1,0:T(8,128)(2,1)}) %all-gather.10.cloned.1.call-update) | async-done | bytes 5767184 | tf_op jit(solution)/shard_map/all_gather | solution.py:295
  575.1 49.3 %all-gather.12.cloned.1.call-done = bf16[1408,2048]{0,1:T(8,128)(2,1)} async-done(((bf16[1408,64]{0,1:T(8,128)(2,1)}), bf16[1408,2048]{0,1:T(8,128)(2,1)}) %all-gather.12.cloned.1.call-update) | async-done | bytes 5767184 | tf_op jit(solution)/shard_map/all_gather | solution.py:299
  624.5 11.2 %convolution_convert_fusion = bf16[384,2048]{1,0:T(8,128)(2,1)} fusion(bf16[1408,2048]{0,1:T(8,128)(2,1)} %all-gather.12.cloned.1.call-done, bf16[384,2048]{1,0:T(8,128)(2,1)S(1)} %copy-done.14, bf16[2048,1408]{1,0:T(8,128)(2,1)} %all-gather.10.cloned.1.call-done, f32[384,1408]{1,0:T(8,128)} %fusion.102), kind=kOutput, calls=%fused_computation.61 | convolution fusion | flops 4433215488 | bytes 16842752 | tf_op jit(solution)/shard_map/dot_general | solution.py:297
  635.7 24.8 %reduce-scatter.2.cloned.1.call-done = bf16[96,2048]{1,0:T(8,128)(2,1)} async-done(((bf16[384,2048]{1,0:T(8,128)(2,1)}), bf16[96,2048]{1,0:T(8,128)(2,1)}) %reduce-scatter.2.cloned.1.call-update) | async-done | bytes 393232 | tf_op jit(solution)/shard_map/reduce_scatter | solution.py:302
  (331 shorter events, 168.2 us)
Async XLA Ops:
  6.5 38.3 %copy-start = (bf16[2048,512]{1,0:T(8,128)(2,1)S(1)}, bf16[2048,512]{1,0:T(8,128)(2,1)}, u32[]{:S(2)}) copy-start(bf16[2048,512]{1,0:T(8,128)(2,1)} %param.29) | copy-start | bytes 6291460
  6.5 260.0 %all-gather.14.cloned.1.call-start = ((), (), s32[]{:S(2)}) async-start(), calls=%async_computation.6 | async-start | bytes 4325376 | tf_op jit(solution)/shard_map/all_gather | solution.py:25
  6.5 12.4 %collective-permute-start = (bf16[96,2048]{1,0:T(8,128)(2,1)}, bf16[96,2048]{1,0:T(8,128)(2,1)S(1)}, u32[]{:S(2)}, u32[]{:S(2)}) collective-permute-start(bf16[96,2048]{1,0:T(8,128)(2,1)} %param.26), channel_id=1, source_target_pairs={{0,1},{1,2},{2,3},{3,0},{4,5},{5,6},{6,7},{7,4},{8,9},{9,10},{10,1... | collective-permute-start | bytes 1179656 | tf_op jit(solution)/shard_map/ppermute | solution.py:188
  8.2 11.2 %collective-permute-start.2 = (bf16[96,2048]{1,0:T(8,128)(2,1)}, bf16[96,2048]{1,0:T(8,128)(2,1)S(1)}, u32[]{:S(2)}, u32[]{:S(2)}) collective-permute-start(bf16[96,2048]{1,0:T(8,128)(2,1)} %param.26), channel_id=1, source_target_pairs={{1,0},{2,1},{3,2},{0,3},{5,4},{6,5},{7,6},{4,7},{9,8},{10,9},{11,1... | collective-permute-start | bytes 1179656 | tf_op jit(solution)/shard_map/ppermute | solution.py:190
  19.0 11.6 %collective-permute-start.1 = (bf16[96,2048]{1,0:T(8,128)(2,1)S(1)}, bf16[96,2048]{1,0:T(8,128)(2,1)}, u32[]{:S(2)}, u32[]{:S(2)}) collective-permute-start(bf16[96,2048]{1,0:T(8,128)(2,1)S(1)} %collective-permute-done), channel_id=1, source_target_pairs={{0,1},{1,2},{2,3},{3,0},{4,5},{5,6},{6,7},{7,4},{8,9},{9,10},{10,1... | collective-permute-start | bytes 1179656 | tf_op jit(solution)/shard_map/ppermute | solution.py:188
  40.2 8.8 %copy-start.3 = (bf16[384,2048]{1,0:T(8,128)(2,1)}, bf16[384,2048]{1,0:T(8,128)(2,1)S(1)}, u32[]{:S(2)}) copy-start(bf16[384,2048]{1,0:T(8,128)(2,1)S(1)} %fusion.44) | copy-start | bytes 4718596
  47.7 6.0 collective-permute-start.3
  60.4 2.9 copy-start.11
  60.4 122.2 %copy-start.16 = (bf16[384,1024]{1,0:T(8,128)(2,1)S(1)}, bf16[384,1024]{1,0:T(8,128)(2,1)}, u32[]{:S(2)}) copy-start(bf16[384,1024]{1,0:T(8,128)(2,1)} %copy-done.15) | copy-start | bytes 2359300
  63.2 119.6 %copy-start.24 = (f32[1,1024]{1,0:T(1,128)S(1)}, f32[1,1024]{1,0:T(1,128)}, u32[]{:S(2)}) copy-start(f32[1,1024]{1,0:T(1,128)} %get-tuple-element.401) | copy-start | bytes 12292
  63.3 119.6 %copy-start.25 = (f32[1,1024]{1,0:T(1,128)S(1)}, f32[1,1024]{1,0:T(1,128)}, u32[]{:S(2)}) copy-start(f32[1,1024]{1,0:T(1,128)} %get-tuple-element.402) | copy-start | bytes 12292
  185.2 2.9 copy-start.12
  218.7 102.2 %all-gather.16.cloned.1.call-start = ((), (), s32[]{:S(2)}) async-start(), calls=%async_computation.7 | async-start | bytes 8650752 | tf_op jit(solution)/shard_map/all_gather | solution.py:25
  219.5 256.0 %all-reduce.2.cloned.1.call-start = ((), (), s32[]{:S(2)}) async-start(), calls=%async_computation.1 | async-start | bytes 3145728 | tf_op jit(solution)/shard_map/psum | solution.py:286
  220.0 4.2 copy-start.9
  425.4 50.1 %copy-start.2 = (bf16[4,96,2048]{2,1,0:T(8,128)(2,1)S(1)}, bf16[4,96,2048]{2,1,0:T(8,128)(2,1)}, u32[]{:S(2)}) copy-start(bf16[4,96,2048]{2,1,0:T(8,128)(2,1)} %gather_fusion) | copy-start | bytes 4718596
  425.4 100.4 %all-gather.8.cloned.1.call-start = ((), (), s32[]{:S(2)}) async-start(), calls=%async_computation.2 | async-start | bytes 5947392 | tf_op jit(solution)/shard_map/all_gather | solution.py:294
  426.0 149.1 %all-gather.10.cloned.1.call-start = ((), (), s32[]{:S(2)}) async-start(), calls=%async_computation.3 | async-start | bytes 5947392 | tf_op jit(solution)/shard_map/all_gather | solution.py:295
  426.6 197.9 %all-gather.12.cloned.1.call-start = ((), (), s32[]{:S(2)}) async-start(), calls=%async_computation.4 | async-start | bytes 5947392 | tf_op jit(solution)/shard_map/all_gather | solution.py:299
  427.1 52.0 %copy-start.27 = (f32[2048]{0:T(1024)S(1)}, f32[2048]{0:T(1024)}, u32[]{:S(2)}) copy-start(f32[2048]{0:T(1024)} %param.42) | copy-start | bytes 24580
  427.2 233.3 %reduce-scatter.2.cloned.1.call-start = ((), (), s32[]{:S(2)}) async-start(), calls=%async_computation.5 | async-start | bytes 1966080 | tf_op jit(solution)/shard_map/reduce_scatter | solution.py:302
  475.5 3.7 copy-start.8
  481.1 143.4 %copy-start.14 = (bf16[384,2048]{1,0:T(8,128)(2,1)S(1)}, bf16[384,2048]{1,0:T(8,128)(2,1)}, u32[]{:S(2)}) copy-start(bf16[384,2048]{1,0:T(8,128)(2,1)} %multiply_convert_fusion) | copy-start | bytes 4718596
  635.7 26.9 %copy-start.1 = (bf16[2048,512]{1,0:T(8,128)(2,1)S(1)}, bf16[2048,512]{1,0:T(8,128)(2,1)}, u32[]{:S(2)}) copy-start(bf16[2048,512]{1,0:T(8,128)(2,1)} %param.29) | copy-start | bytes 6291460
  (32 other events, 63.2 us)
Sparse Core Ops, SparseCore 0:
  218.8 47.6 all-gather.13
  268.8 52.1 all-gather.15
  425.5 49.9 all-reduce.1
  477.6 48.1 all-gather.7
  527.9 47.1 all-gather.9
  577.2 47.1 all-gather.11
  635.8 24.6 reduce-scatter.1
